TPU v7x, 256 devices: a whole 4x4x8 slice. The times are simulated.
256 devices in a mesh: dm: 32 (over x_lo, z, core), beam: 8 (over y, x_hi).
Axes of the slice: x: 4 (x_hi: 2, x_lo: 2; x = x_hi * 2 + x_lo), y: 4, z: 8, core: 2. Of those that a mesh axis runs over, the one named last changes fastest.
Arguments:
- voltages: bfloat16 [4096, 8, 2, 256], P(('beam', 'dm')), may hold values from -6 to 6
- responses: bfloat16 [128, 4096, 2, 256], P('dm', 'beam'), may hold values from -6 to 6
- chirp_len: int32 [128], P('dm'), may hold values from 1 to 128, as said below
Outputs:
- detected: bfloat16 [128, 8, 262144], P('dm', 'beam')
Inputs may be any that keep to these rules, and one draw needn't show every extreme that they name: `chirp_len`: some trial has the longest chirp 256 // 2 and some trial a chirp of 1 sample.
All inputs are finite; a program needn't handle non-finite values.
Results may differ from a plain program's by a relative error of at most 0.0054.
Values may be sent and summed in bfloat16 or wider, within the bound.
No kernel may reach another device: no remote copies, remote signals or barrier semaphores. Data moves between devices by JAX's collectives and lax.ppermute only.
A program may use at most 128 MiB of HBM per device.

v0:
```python
import math
import jax
import jax.numpy as jnp
from jax import lax
from jax.sharding import PartitionSpec as P

RATE = 4


def dft_tables(length):
    sample = jnp.arange(length, dtype=jnp.int32)
    phases = sample[:, None] * sample[None, :] % length
    angles = phases.astype(jnp.float32) * (2.0 * math.pi / length)
    cosine = jnp.cos(angles) / math.sqrt(length)
    sine_part = jnp.sin(angles) / math.sqrt(length)
    forward = jnp.concatenate(
        [jnp.concatenate([cosine, -sine_part], 1), jnp.concatenate([sine_part, cosine], 1)], 0
    )
    backward = jnp.concatenate(
        [jnp.concatenate([cosine, sine_part], 1), jnp.concatenate([-sine_part, cosine], 1)], 0
    )
    return (forward.astype(jnp.bfloat16), backward.astype(jnp.bfloat16))


def spectrum(signal, forward):
    length = signal.shape[-1]
    flattened = signal.reshape(-1, 2 * length)
    result = jnp.dot(flattened, forward, preferred_element_type=jnp.float32)
    return result.astype(jnp.bfloat16).reshape(signal.shape)


def detect(spectra, response, lengths, backward, rate):
    chans = spectra.shape[0]
    beam_count = spectra.shape[1]
    length = spectra.shape[-1]
    samples_out = length // rate
    spec_re = spectra[:, :, 0, :].astype(jnp.float32)
    spec_im = spectra[:, :, 1, :].astype(jnp.float32)
    sample = jnp.arange(length, dtype=jnp.int32)

    def one_trial(trial):
        filter_row, chirp = trial
        resp_re = filter_row[:, 0, :].astype(jnp.float32)[:, None, :]
        resp_im = filter_row[:, 1, :].astype(jnp.float32)[:, None, :]
        real_part = resp_re * spec_re - resp_im * spec_im
        imag_part = resp_re * spec_im + resp_im * spec_re
        joined = jnp.concatenate([real_part, imag_part], -1).astype(jnp.bfloat16)
        series = jnp.dot(
            joined.reshape(-1, 2 * length), backward, preferred_element_type=jnp.float32
        )
        series = series.reshape(chans, beam_count, 2 * length)
        powers = series[..., :length] ** 2 + series[..., length:] ** 2
        valid_mask = sample >= chirp
        powers = jnp.where(valid_mask[None, None, :], powers, jnp.float32(0.0))
        binned = powers.reshape(chans, beam_count, samples_out, rate).sum(-1) / rate
        return jnp.transpose(binned, (1, 0, 2)).astype(jnp.bfloat16)

    return lax.map(one_trial, (response, lengths))


def shards(voltages, responses, chirp_len):
    length = voltages.shape[-1]
    forward, backward = dft_tables(length)
    trial_count = responses.shape[0]
    prepared = spectrum(lax.all_gather(voltages, "dm", axis=0, tiled=True), forward)
    detected = detect(prepared, responses, chirp_len, backward, RATE)
    flattened = detected.reshape(trial_count, detected.shape[1], -1)
    return lax.all_to_all(flattened, "beam", split_axis=1, concat_axis=2, tiled=True)


def solution(mesh):
    placed = (P(("beam", "dm"), None, None, None), P("dm", "beam", None, None), P("dm"))
    return jax.shard_map(
        shards, mesh=mesh, in_specs=placed, out_specs=P("dm", "beam", None), check_vma=False
    )
```

profile of v0, /device:TPU:1, one launch (start us, length us, event | category | flops | bytes accessed | tf_op | source)
XLA Modules:
  0.0 263.4 jit_solution(4098460005403602583)
XLA Ops:
  11.1 68.8 %all-gather.2.cloned.1.call-done = bf16[512,8,2,256]{3,1,2,0:T(8,128)(2,1)} async-done(((bf16[16,8,2,256]{3,1,2,0:T(8,128)(2,1)}), bf16[512,8,2,256]{3,1,2,0:T(8,128)(2,1)}) %all-gather.2.cloned.1.call-update) | async-done | bytes 4194320 | tf_op jit(solution)/shard_map/all_gather | solution.py:65
  79.9 6.5 %fusion.14 = bf16[4096,512]{0,1:T(8,128)(2,1)} fusion(bf16[4096,512]{1,0:T(8,128)(2,1)} %bitcast.54, bf16[256,256]{0,1:T(8,128)(2,1)S(1)} %get-tuple-element.106, bf16[256,256]{0,1:T(8,128)(2,1)S(1)} %fusion.26, bf16[256,256]{0,1:T(8,128)(2,1)S(1)} %get-tuple-element.105), kind=kOutput, calls=%fused_computation.24 | convolution fusion | flops 2151677952 | bytes 8781824 | tf_op jit(solution)/shard_map/dot_general | solution.py:28
  86.4 6.5 %copy.12 = bf16[4096,512]{1,0:T(8,128)(2,1)} copy(bf16[4096,512]{0,1:T(8,128)(2,1)} %fusion.14) | data formatting | bytes 8388608 | tf_op jit(solution)/shard_map/convert_element_type | solution.py:29
  92.9 7.0 %reshape.32 = bf16[512,8,2,256]{3,2,1,0:T(2,128)(2,1)} reshape(bf16[4096,512]{1,0:T(8,128)(2,1)} %copy.12) | data formatting | bytes 8388608 | tf_op jit(solution)/shard_map/reshape | solution.py:29
  99.9 8.8 %slice_convert_fusion = (f32[512,8,1,256]{3,2,1,0:T(1,128)S(1)}, f32[512,8,1,256]{3,2,1,0:T(1,128)S(1)}) fusion(bf16[512,8,2,256]{3,2,1,0:T(2,128)(2,1)} %reshape.32), kind=kLoop, calls=%fused_computation.25 | loop fusion | flops 2097152 | bytes 12582912 | tf_op jit(solution)/shard_map/convert_element_type | solution.py:38
  115.2 96.9 %while.11 = (s32[]{:T(128)}, bf16[4,8,512,64]{2,3,1,0:T(8,128)(2,1)S(1)}, s32[4]{0:T(128)S(1)}, bf16[4,512,2,256]{3,2,1,0:T(2,128)(2,1)}, f32[512,8,256]{2,0,1:T...) while((s32[]{:T(128)}, ...), condition=%wide.region_2.3_spmd.clone, body=%wide.region_0.2_spmd.clone.sunk | while | flops 2170028288 | bytes 58196600 | solution.py:58
  116.7 4.8 %subtract_convert_fusion.2 = (bf16[512,8,256]{2,0,1:T(8,128)(2,1)S(1)}, bf16[512,8,256]{2,0,1:T(8,128)(2,1)S(1)}) fusion(f32[512,8,256]{2,0,1:T(8,128)} %get-tuple-element.181, f32[512,8,256]{2,0,1:T(8,128)} %get-tuple-element.180, f32[512,256]{1,0:T(8,128)S(1)} %get-tuple-element.154, f32[512,256]{1,0:T(8,128)S(1)} %get-tuple-element.155), kind=kLoop, calls=%fused_computation.10.clone.1 | loop fusion | flops 8388608 | bytes 13631488 | tf_op jit(solution)/shard_map/convert.2
  121.5 3.4 %fusion.38 = f32[512,8,512]{0,2,1:T(8,128)S(1)} fusion(bf16[512,8,256]{2,0,1:T(8,128)(2,1)S(1)} %get-tuple-element.156, bf16[512,8,256]{2,0,1:T(8,128)(2,1)S(1)} %get-tuple-element.157, bf16[512,512]{0,1:T(8,128)(2,1)} %get-tuple-element.182), kind=kOutput, calls=%fused_computation.5.clone.1 | convolution fusion | flops 2155872256 | bytes 13107200 | tf_op jit(solution)/shard_map/while/body/eval_jaxpr/dot_general | solution.py:48
  129.3 5.2 %reshape.44 = f32[512,8,64,4]{0,3,2,1:T(4,128)} reshape(f32[512,8,256]{0,2,1:T(8,128)} %fusion.39) | data formatting | bytes 8388608 | tf_op jit(solution)/shard_map/while/body/eval_jaxpr/reshape | solution.py:55
  134.5 4.8 %reduce_sum.11 = f32[512,8,64]{0,2,1:T(8,128)S(1)} reduce(f32[512,8,64,4]{0,3,2,1:T(4,128)} %reshape.44, f32[]{:T(128)} %constant.29.clone.3..sunk), dimensions={3}, to_apply=%region_1.1 | reduce | flops 786432 | bytes 5242884 | tf_op jit(solution)/shard_map/while/body/eval_jaxpr/reduce_sum | solution.py:55
  141.0 4.8 %subtract_convert_fusion.2 = (bf16[512,8,256]{2,0,1:T(8,128)(2,1)S(1)}, bf16[512,8,256]{2,0,1:T(8,128)(2,1)S(1)}) fusion(f32[512,8,256]{2,0,1:T(8,128)} %get-tuple-element.181, f32[512,8,256]{2,0,1:T(8,128)} %get-tuple-element.180, f32[512,256]{1,0:T(8,128)S(1)} %get-tuple-element.154, f32[512,256]{1,0:T(8,128)S(1)} %get-tuple-element.155), kind=kLoop, calls=%fused_computation.10.clone.1 | loop fusion | flops 8388608 | bytes 13631488 | tf_op jit(solution)/shard_map/convert.2
  145.8 3.4 %fusion.38 = f32[512,8,512]{0,2,1:T(8,128)S(1)} fusion(bf16[512,8,256]{2,0,1:T(8,128)(2,1)S(1)} %get-tuple-element.156, bf16[512,8,256]{2,0,1:T(8,128)(2,1)S(1)} %get-tuple-element.157, bf16[512,512]{0,1:T(8,128)(2,1)} %get-tuple-element.182), kind=kOutput, calls=%fused_computation.5.clone.1 | convolution fusion | flops 2155872256 | bytes 13107200 | tf_op jit(solution)/shard_map/while/body/eval_jaxpr/dot_general | solution.py:48
  153.5 5.2 %reshape.44 = f32[512,8,64,4]{0,3,2,1:T(4,128)} reshape(f32[512,8,256]{0,2,1:T(8,128)} %fusion.39) | data formatting | bytes 8388608 | tf_op jit(solution)/shard_map/while/body/eval_jaxpr/reshape | solution.py:55
  158.7 4.8 %reduce_sum.11 = f32[512,8,64]{0,2,1:T(8,128)S(1)} reduce(f32[512,8,64,4]{0,3,2,1:T(4,128)} %reshape.44, f32[]{:T(128)} %constant.29.clone.3..sunk), dimensions={3}, to_apply=%region_1.1 | reduce | flops 786432 | bytes 5242884 | tf_op jit(solution)/shard_map/while/body/eval_jaxpr/reduce_sum | solution.py:55
  165.2 4.8 %subtract_convert_fusion.2 = (bf16[512,8,256]{2,0,1:T(8,128)(2,1)S(1)}, bf16[512,8,256]{2,0,1:T(8,128)(2,1)S(1)}) fusion(f32[512,8,256]{2,0,1:T(8,128)} %get-tuple-element.181, f32[512,8,256]{2,0,1:T(8,128)} %get-tuple-element.180, f32[512,256]{1,0:T(8,128)S(1)} %get-tuple-element.154, f32[512,256]{1,0:T(8,128)S(1)} %get-tuple-element.155), kind=kLoop, calls=%fused_computation.10.clone.1 | loop fusion | flops 8388608 | bytes 13631488 | tf_op jit(solution)/shard_map/convert.2
  170.0 3.4 %fusion.38 = f32[512,8,512]{0,2,1:T(8,128)S(1)} fusion(bf16[512,8,256]{2,0,1:T(8,128)(2,1)S(1)} %get-tuple-element.156, bf16[512,8,256]{2,0,1:T(8,128)(2,1)S(1)} %get-tuple-element.157, bf16[512,512]{0,1:T(8,128)(2,1)} %get-tuple-element.182), kind=kOutput, calls=%fused_computation.5.clone.1 | convolution fusion | flops 2155872256 | bytes 13107200 | tf_op jit(solution)/shard_map/while/body/eval_jaxpr/dot_general | solution.py:48
  177.8 5.2 %reshape.44 = f32[512,8,64,4]{0,3,2,1:T(4,128)} reshape(f32[512,8,256]{0,2,1:T(8,128)} %fusion.39) | data formatting | bytes 8388608 | tf_op jit(solution)/shard_map/while/body/eval_jaxpr/reshape | solution.py:55
  183.0 4.8 %reduce_sum.11 = f32[512,8,64]{0,2,1:T(8,128)S(1)} reduce(f32[512,8,64,4]{0,3,2,1:T(4,128)} %reshape.44, f32[]{:T(128)} %constant.29.clone.3..sunk), dimensions={3}, to_apply=%region_1.1 | reduce | flops 786432 | bytes 5242884 | tf_op jit(solution)/shard_map/while/body/eval_jaxpr/reduce_sum | solution.py:55
  189.5 4.8 %subtract_convert_fusion.2 = (bf16[512,8,256]{2,0,1:T(8,128)(2,1)S(1)}, bf16[512,8,256]{2,0,1:T(8,128)(2,1)S(1)}) fusion(f32[512,8,256]{2,0,1:T(8,128)} %get-tuple-element.181, f32[512,8,256]{2,0,1:T(8,128)} %get-tuple-element.180, f32[512,256]{1,0:T(8,128)S(1)} %get-tuple-element.154, f32[512,256]{1,0:T(8,128)S(1)} %get-tuple-element.155), kind=kLoop, calls=%fused_computation.10.clone.1 | loop fusion | flops 8388608 | bytes 13631488 | tf_op jit(solution)/shard_map/convert.2
  194.2 3.4 %fusion.38 = f32[512,8,512]{0,2,1:T(8,128)S(1)} fusion(bf16[512,8,256]{2,0,1:T(8,128)(2,1)S(1)} %get-tuple-element.156, bf16[512,8,256]{2,0,1:T(8,128)(2,1)S(1)} %get-tuple-element.157, bf16[512,512]{0,1:T(8,128)(2,1)} %get-tuple-element.182), kind=kOutput, calls=%fused_computation.5.clone.1 | convolution fusion | flops 2155872256 | bytes 13107200 | tf_op jit(solution)/shard_map/while/body/eval_jaxpr/dot_general | solution.py:48
  202.0 5.2 %reshape.44 = f32[512,8,64,4]{0,3,2,1:T(4,128)} reshape(f32[512,8,256]{0,2,1:T(8,128)} %fusion.39) | data formatting | bytes 8388608 | tf_op jit(solution)/shard_map/while/body/eval_jaxpr/reshape | solution.py:55
  207.2 4.8 %reduce_sum.11 = f32[512,8,64]{0,2,1:T(8,128)S(1)} reduce(f32[512,8,64,4]{0,3,2,1:T(4,128)} %reshape.44, f32[]{:T(128)} %constant.29.clone.3..sunk), dimensions={3}, to_apply=%region_1.1 | reduce | flops 786432 | bytes 5242884 | tf_op jit(solution)/shard_map/while/body/eval_jaxpr/reduce_sum | solution.py:55
  215.3 6.3 %reshape.42 = bf16[4,8,32768]{2,0,1:T(4,128)(2,1)S(1)} reshape(bf16[4,8,512,64]{3,2,0,1:T(8,128)(2,1)} %copy.20) | data formatting | bytes 4194304 | tf_op jit(solution)/shard_map/reshape | solution.py:67
  221.6 33.6 %all_to_all.12 = bf16[4,8,32768]{2,0,1:T(4,128)(2,1)S(1)} all-to-all(bf16[4,8,32768]{2,0,1:T(4,128)(2,1)S(1)} %reshape.42), channel_id=1, replica_groups=mesh['dm'=32,'beam'=8] {'beam'}, dimensions={1} | all-to-all | bytes 4194304 | tf_op jit(solution)/shard_map/all_to_all | solution.py:68
  (41 shorter events, 39.7 us)
Async XLA Ops:
  6.5 73.4 %all-gather.2.cloned.1.call-start = ((), (), s32[]{:S(2)}) async-start(), calls=%async_computation.1 | async-start | bytes 4325376 | tf_op jit(solution)/shard_map/all_gather | solution.py:65
  111.9 3.2 %copy-start = (s32[4]{0:T(128)S(1)}, s32[4]{0:T(128)}, u32[]{:S(2)}) copy-start(s32[4]{0:T(128)} %param.7) | copy-start | bytes 52
Sparse Core Ops, SparseCore 0:
  9.2 70.6 all-gather.1
where the time goes:
time: 265 us; the launch traced here: 263 us
  waiting for transfers between devices  68.8 us (26%)
  other arithmetic  65.7 us (25%)
  local copies, waits for them, and re-layouts  61.3 us (23%)
  blocking collectives  33.6 us (13%)
  matrix products  20.2 us (8%)
  between operations  13.4 us (5%)
    all_gather x1, waiting for transfers between devices, shards(): lax.all_gather(voltages, 'dm', axis=0, tiled=True)  68.8 us
    all_to_all x1, blocking collectives, shards(): lax.all_to_all(flattened, 'beam', split_axis=1, concat_axis=2, tiled=True)  33.6 us
    another operation x6, other arithmetic  21.1 us
    reshape x4, local copies, waits for them, and re-layouts, one_trial(): binned = powers.reshape(chans, beam_count, samples_out, rate).sum(-1) / rate  20.7 us
    reduce_sum x4, other arithmetic, one_trial(): binned = powers.reshape(chans, beam_count, samples_out, rate).sum(-1) / rate  19.1 us
    dot_general x4, matrix products, one_trial(): jnp.dot(joined.reshape(-1, 2 * length), backward, preferred_element_type=...  13.7 us
    select_n x4, other arithmetic, one_trial(): powers = jnp.where(valid_mask[None, None, :], powers, jnp.float32(0.0))  12.5 us
    reshape x2, local copies, waits for them, and re-layouts, shards(): flattened = detected.reshape(trial_count, detected.shape[1], -1)  9.45 us
  transfers between devices with their start and end apart: 1, of which 1 were waited for; matrix products, arithmetic and copies ran while one was open for 1% of the time, Pallas kernels for 0%

commit v1 on v0

--- a/solution.py
+++ b/solution.py
@@ -62,7 +62,12 @@
     length = voltages.shape[-1]
     forward, backward = dft_tables(length)
     trial_count = responses.shape[0]
-    prepared = spectrum(lax.all_gather(voltages, "dm", axis=0, tiled=True), forward)
+    prepared = spectrum(
+        jnp.concatenate(
+            lax.all_to_all(jnp.stack([voltages] * lax.axis_size("dm")), "dm", 0, 0), axis=0
+        ),
+        forward,
+    )
     detected = detect(prepared, responses, chirp_len, backward, RATE)
     flattened = detected.reshape(trial_count, detected.shape[1], -1)
     return lax.all_to_all(flattened, "beam", split_axis=1, concat_axis=2, tiled=True)

time: 265 us -> 291 us (1.098)
  waiting for transfers between devices: 68.8 us -> 91.7 us
  between operations: 13.4 us -> 0.06 us
  starting transfers between devices: 0.01 us -> 11.1 us
  local copies, waits for them, and re-layouts: 61.3 us -> 69.4 us
    all_to_all x0 -> x1, waiting for transfers between devices: none -> 91.7 us  [shards(): lax.all_to_all(jnp.stack([voltages] * lax.axis_size('dm')), 'dm', 0, 0)]
    all_gather x1 -> x0, waiting for transfers between devices: 68.8 us -> none  [shards(): lax.all_gather(voltages, 'dm', axis=0, tiled=True)]
    all_to_all x0 -> x1, starting transfers between devices: none -> 11.1 us  [shards(): lax.all_to_all(jnp.stack([voltages] * lax.axis_size('dm')), 'dm', 0, 0)]
    another operation x0 -> x1, local copies, waits for them, and re-layouts: none -> 6.66 us  [shards(): jnp.stack([voltages] * lax.axis_size('dm'))]
where the time goes in v1:
time: 291 us; the launch traced here: 290 us
  waiting for transfers between devices  91.7 us (32%)
  local copies, waits for them, and re-layouts  69.4 us (24%)
  other arithmetic  65.6 us (23%)
  blocking collectives  33.6 us (12%)
  matrix products  18 us (6%)
  starting transfers between devices  11.1 us (4%)
    all_to_all x1, waiting for transfers between devices, shards(): lax.all_to_all(jnp.stack([voltages] * lax.axis_size('dm')), 'dm', 0, 0)  91.7 us
    all_to_all x1, blocking collectives, shards(): lax.all_to_all(flattened, 'beam', split_axis=1, concat_axis=2, tiled=True)  33.6 us
    another operation x6, other arithmetic  21.1 us
    reshape x4, local copies, waits for them, and re-layouts, one_trial(): binned = powers.reshape(chans, beam_count, samples_out, rate).sum(-1) / rate  20.7 us
    reduce_sum x4, other arithmetic, one_trial(): binned = powers.reshape(chans, beam_count, samples_out, rate).sum(-1) / rate  19.1 us
    dot_general x4, matrix products, one_trial(): jnp.dot(joined.reshape(-1, 2 * length), backward, preferred_element_type=...  13.7 us
    select_n x4, other arithmetic, one_trial(): powers = jnp.where(valid_mask[None, None, :], powers, jnp.float32(0.0))  12.4 us
    all_to_all x1, starting transfers between devices, shards(): lax.all_to_all(jnp.stack([voltages] * lax.axis_size('dm')), 'dm', 0, 0)  11.1 us
  transfers between devices with their start and end apart: 1, of which 1 were waited for; matrix products, arithmetic and copies ran while one was open for 1% of the time, Pallas kernels for 0%

profile of v1, /device:TPU:1, one launch (start us, length us, event | category | flops | bytes accessed | tf_op | source)
XLA Modules:
  0.0 289.8 jit_solution(7090966554814448251)
XLA Ops:
  0.0 6.7 %stack.2 = bf16[32,16,8,2,256]{4,3,2,1,0:T(2,128)(2,1)} broadcast(bf16[16,8,2,256]{3,2,1,0:T(2,128)(2,1)} %param.5), dimensions={1,2,3,4} | broadcast | bytes 4325376 | tf_op jit(solution)/shard_map/stack | solution.py:67
  6.7 11.1 %all-to-all-start = ((bf16[32,16,8,2,256]{4,3,2,1,0:T(2,128)(2,1)}), bf16[32,16,8,2,256]{4,3,2,1,0:T(2,128)(2,1)}, u32[]{:S(2)}, u32[]{:S(2)}) async-start(bf16[32,16,8,2,256]{4,3,2,1,0:T(2,128)(2,1)} %stack.2), calls=%async_computation | async-start | bytes 8388608 | tf_op jit(solution)/shard_map/all_to_all | solution.py:67
  20.7 91.7 %all-to-all-done = bf16[32,16,8,2,256]{4,3,2,1,0:T(2,128)(2,1)} async-done(((bf16[32,16,8,2,256]{4,3,2,1,0:T(2,128)(2,1)}), bf16[32,16,8,2,256]{4,3,2,1,0:T(2,128)(2,1)}, u32[]{:S(2)}, u32[]{:S(2)}) %all-to-all-start) | async-done | bytes 4194336 | tf_op jit(solution)/shard_map/all_to_all | solution.py:67
  115.4 4.4 %fusion.14 = bf16[4096,512]{0,1:T(8,128)(2,1)} fusion(bf16[4096,512]{1,0:T(8,128)(2,1)S(1)} %bitcast.56, bf16[256,256]{0,1:T(8,128)(2,1)S(1)} %get-tuple-element.106, bf16[256,256]{0,1:T(8,128)(2,1)S(1)} %fusion.26, bf16[256,256]{0,1:T(8,128)(2,1)S(1)} %get-tuple-element.105), kind=kOutput, calls=%fused_computation.24 | convolution fusion | flops 2151677952 | bytes 8781824 | tf_op jit(solution)/shard_map/dot_general | solution.py:28
  119.7 6.5 %copy.11 = bf16[4096,512]{1,0:T(8,128)(2,1)} copy(bf16[4096,512]{0,1:T(8,128)(2,1)} %fusion.14) | data formatting | bytes 8388608 | tf_op jit(solution)/shard_map/convert_element_type | solution.py:29
  126.2 7.0 %reshape.30 = bf16[512,8,2,256]{3,2,1,0:T(2,128)(2,1)} reshape(bf16[4096,512]{1,0:T(8,128)(2,1)} %copy.11) | data formatting | bytes 8388608 | tf_op jit(solution)/shard_map/reshape | solution.py:29
  133.2 8.8 %slice_convert_fusion = (f32[512,8,1,256]{3,2,1,0:T(1,128)S(1)}, f32[512,8,1,256]{3,2,1,0:T(1,128)S(1)}) fusion(bf16[512,8,2,256]{3,2,1,0:T(2,128)(2,1)} %reshape.30), kind=kLoop, calls=%fused_computation.25 | loop fusion | flops 2097152 | bytes 12582912 | tf_op jit(solution)/shard_map/convert_element_type | solution.py:38
  148.5 97.0 %while.11 = (s32[]{:T(128)}, bf16[4,8,512,64]{2,3,1,0:T(8,128)(2,1)S(1)}, s32[4]{0:T(128)S(1)}, bf16[4,512,2,256]{3,2,1,0:T(2,128)(2,1)}, f32[512,8,256]{2,0,1:T...) while((s32[]{:T(128)}, ...), condition=%wide.region_2.3_spmd.clone, body=%wide.region_0.2_spmd.clone.sunk | while | flops 2170028288 | bytes 58196600 | solution.py:58
  150.0 4.8 %subtract_convert_fusion.2 = (bf16[512,8,256]{2,0,1:T(8,128)(2,1)S(1)}, bf16[512,8,256]{2,0,1:T(8,128)(2,1)S(1)}) fusion(f32[512,8,256]{2,0,1:T(8,128)} %get-tuple-element.181, f32[512,8,256]{2,0,1:T(8,128)} %get-tuple-element.180, f32[512,256]{1,0:T(8,128)S(1)} %get-tuple-element.154, f32[512,256]{1,0:T(8,128)S(1)} %get-tuple-element.155), kind=kLoop, calls=%fused_computation.10.clone.1 | loop fusion | flops 8388608 | bytes 13631488 | tf_op jit(solution)/shard_map/convert.2
  162.6 5.2 %reshape.42 = f32[512,8,64,4]{0,3,2,1:T(4,128)} reshape(f32[512,8,256]{0,2,1:T(8,128)} %fusion.39) | data formatting | bytes 8388608 | tf_op jit(solution)/shard_map/while/body/eval_jaxpr/reshape | solution.py:55
  167.8 4.8 %reduce_sum.11 = f32[512,8,64]{0,2,1:T(8,128)S(1)} reduce(f32[512,8,64,4]{0,3,2,1:T(4,128)} %reshape.42, f32[]{:T(128)} %constant.29.clone.3..sunk), dimensions={3}, to_apply=%region_1.1 | reduce | flops 786432 | bytes 5242884 | tf_op jit(solution)/shard_map/while/body/eval_jaxpr/reduce_sum | solution.py:55
  174.3 4.8 %subtract_convert_fusion.2 = (bf16[512,8,256]{2,0,1:T(8,128)(2,1)S(1)}, bf16[512,8,256]{2,0,1:T(8,128)(2,1)S(1)}) fusion(f32[512,8,256]{2,0,1:T(8,128)} %get-tuple-element.181, f32[512,8,256]{2,0,1:T(8,128)} %get-tuple-element.180, f32[512,256]{1,0:T(8,128)S(1)} %get-tuple-element.154, f32[512,256]{1,0:T(8,128)S(1)} %get-tuple-element.155), kind=kLoop, calls=%fused_computation.10.clone.1 | loop fusion | flops 8388608 | bytes 13631488 | tf_op jit(solution)/shard_map/convert.2
  179.0 3.4 %fusion.38 = f32[512,8,512]{0,2,1:T(8,128)S(1)} fusion(bf16[512,8,256]{2,0,1:T(8,128)(2,1)S(1)} %get-tuple-element.156, bf16[512,8,256]{2,0,1:T(8,128)(2,1)S(1)} %get-tuple-element.157, bf16[512,512]{0,1:T(8,128)(2,1)} %get-tuple-element.182), kind=kOutput, calls=%fused_computation.5.clone.1 | convolution fusion | flops 2155872256 | bytes 13107200 | tf_op jit(solution)/shard_map/while/body/eval_jaxpr/dot_general | solution.py:48
  186.9 5.2 %reshape.42 = f32[512,8,64,4]{0,3,2,1:T(4,128)} reshape(f32[512,8,256]{0,2,1:T(8,128)} %fusion.39) | data formatting | bytes 8388608 | tf_op jit(solution)/shard_map/while/body/eval_jaxpr/reshape | solution.py:55
  192.0 4.8 %reduce_sum.11 = f32[512,8,64]{0,2,1:T(8,128)S(1)} reduce(f32[512,8,64,4]{0,3,2,1:T(4,128)} %reshape.42, f32[]{:T(128)} %constant.29.clone.3..sunk), dimensions={3}, to_apply=%region_1.1 | reduce | flops 786432 | bytes 5242884 | tf_op jit(solution)/shard_map/while/body/eval_jaxpr/reduce_sum | solution.py:55
  198.5 4.8 %subtract_convert_fusion.2 = (bf16[512,8,256]{2,0,1:T(8,128)(2,1)S(1)}, bf16[512,8,256]{2,0,1:T(8,128)(2,1)S(1)}) fusion(f32[512,8,256]{2,0,1:T(8,128)} %get-tuple-element.181, f32[512,8,256]{2,0,1:T(8,128)} %get-tuple-element.180, f32[512,256]{1,0:T(8,128)S(1)} %get-tuple-element.154, f32[512,256]{1,0:T(8,128)S(1)} %get-tuple-element.155), kind=kLoop, calls=%fused_computation.10.clone.1 | loop fusion | flops 8388608 | bytes 13631488 | tf_op jit(solution)/shard_map/convert.2
  211.1 5.2 %reshape.42 = f32[512,8,64,4]{0,3,2,1:T(4,128)} reshape(f32[512,8,256]{0,2,1:T(8,128)} %fusion.39) | data formatting | bytes 8388608 | tf_op jit(solution)/shard_map/while/body/eval_jaxpr/reshape | solution.py:55
  216.3 4.8 %reduce_sum.11 = f32[512,8,64]{0,2,1:T(8,128)S(1)} reduce(f32[512,8,64,4]{0,3,2,1:T(4,128)} %reshape.42, f32[]{:T(128)} %constant.29.clone.3..sunk), dimensions={3}, to_apply=%region_1.1 | reduce | flops 786432 | bytes 5242884 | tf_op jit(solution)/shard_map/while/body/eval_jaxpr/reduce_sum | solution.py:55
  222.8 4.8 %subtract_convert_fusion.2 = (bf16[512,8,256]{2,0,1:T(8,128)(2,1)S(1)}, bf16[512,8,256]{2,0,1:T(8,128)(2,1)S(1)}) fusion(f32[512,8,256]{2,0,1:T(8,128)} %get-tuple-element.181, f32[512,8,256]{2,0,1:T(8,128)} %get-tuple-element.180, f32[512,256]{1,0:T(8,128)S(1)} %get-tuple-element.154, f32[512,256]{1,0:T(8,128)S(1)} %get-tuple-element.155), kind=kLoop, calls=%fused_computation.10.clone.1 | loop fusion | flops 8388608 | bytes 13631488 | tf_op jit(solution)/shard_map/convert.2
  227.6 3.4 %fusion.38 = f32[512,8,512]{0,2,1:T(8,128)S(1)} fusion(bf16[512,8,256]{2,0,1:T(8,128)(2,1)S(1)} %get-tuple-element.156, bf16[512,8,256]{2,0,1:T(8,128)(2,1)S(1)} %get-tuple-element.157, bf16[512,512]{0,1:T(8,128)(2,1)} %get-tuple-element.182), kind=kOutput, calls=%fused_computation.5.clone.1 | convolution fusion | flops 2155872256 | bytes 13107200 | tf_op jit(solution)/shard_map/while/body/eval_jaxpr/dot_general | solution.py:48
  235.4 5.2 %reshape.42 = f32[512,8,64,4]{0,3,2,1:T(4,128)} reshape(f32[512,8,256]{0,2,1:T(8,128)} %fusion.39) | data formatting | bytes 8388608 | tf_op jit(solution)/shard_map/while/body/eval_jaxpr/reshape | solution.py:55
  240.5 4.8 %reduce_sum.11 = f32[512,8,64]{0,2,1:T(8,128)S(1)} reduce(f32[512,8,64,4]{0,3,2,1:T(4,128)} %reshape.42, f32[]{:T(128)} %constant.29.clone.3..sunk), dimensions={3}, to_apply=%region_1.1 | reduce | flops 786432 | bytes 5242884 | tf_op jit(solution)/shard_map/while/body/eval_jaxpr/reduce_sum | solution.py:55
  248.6 6.3 %reshape.40 = bf16[4,8,32768]{2,0,1:T(4,128)(2,1)S(1)} reshape(bf16[4,8,512,64]{3,2,0,1:T(8,128)(2,1)} %copy.19) | data formatting | bytes 4194304 | tf_op jit(solution)/shard_map/reshape | solution.py:72
  254.9 33.6 %all_to_all.17 = bf16[4,8,32768]{2,0,1:T(4,128)(2,1)S(1)} all-to-all(bf16[4,8,32768]{2,0,1:T(4,128)(2,1)S(1)} %reshape.40), channel_id=1, replica_groups=mesh['dm'=32,'beam'=8] {'beam'}, dimensions={1} | all-to-all | bytes 4194304 | tf_op jit(solution)/shard_map/all_to_all | solution.py:73
  (41 shorter events, 47.9 us)
Async XLA Ops:
  6.7 105.8 %all-to-all-start = ((bf16[32,16,8,2,256]{4,3,2,1,0:T(2,128)(2,1)}), bf16[32,16,8,2,256]{4,3,2,1,0:T(2,128)(2,1)}, u32[]{:S(2)}, u32[]{:S(2)}) async-start(bf16[32,16,8,2,256]{4,3,2,1,0:T(2,128)(2,1)} %stack.2), calls=%async_computation | async-start | bytes 8388608 | tf_op jit(solution)/shard_map/all_to_all | solution.py:67
  145.2 3.2 %copy-start = (s32[4]{0:T(128)S(1)}, s32[4]{0:T(128)}, u32[]{:S(2)}) copy-start(s32[4]{0:T(128)} %param.7) | copy-start | bytes 52
